TPU v7x, 32 devices: a whole 2x2x4 slice. The times are simulated.
32 devices in a mesh: dp: 4 (over z), pipe: 2 (over core), expert: 4 (over y, x).
Axes of the slice: x: 2, y: 2, z: 4, core: 2. Of those that a mesh axis runs over, the one named last changes fastest.
Arguments:
- tokens: bfloat16 [2, 96, 3072], P(None, 'expert'), may hold values from -6 to 6
- expert_ids: int32 [2, 2, 96, 2], P('pipe', None, 'expert'), may hold values from 0 to 3, all different within a row; in each aligned block of 24 rows (0 to 23, 24 to 47, ..., all dimensions but the last counted through in order) at most 16 rows name the same one
- gates: float32 [2, 2, 96, 2], P('pipe', None, 'expert'), may hold values from 0.1 to 1
- w_gate: bfloat16 [2, 4, 3072, 704], P('pipe', 'expert', None, 'dp'), may hold values from -0.109375 to 0.109375
- w_up: bfloat16 [2, 4, 3072, 704], P('pipe', 'expert', None, 'dp'), may hold values from -0.109375 to 0.109375
- w_down: bfloat16 [2, 4, 704, 3072], P('pipe', 'expert', 'dp'), may hold values from -0.3125 to 0.3125
Outputs:
- layer_out: bfloat16 [2, 2, 96, 3072], P('pipe', None, 'expert', 'dp')
Inputs may be any that keep to these rules, and one draw needn't show every extreme that they name: `expert_ids`: each token names 2 different experts in each layer. Among the tokens of one index of expert in one layer and micro-batch (aligned blocks of 24 tokens) no expert is named by more than 16 tokens, and in some block an expert is named by exactly 16.
All inputs are finite; a program needn't handle non-finite values.
Results may differ from a plain program's by a relative error of at most 0.0052.
Values may be sent and summed in bfloat16 or wider, within the bound.
No kernel may reach another device: no remote copies, remote signals or barrier semaphores. Data moves between devices by JAX's collectives and lax.ppermute only.
A program may use at most 64 MiB of HBM per device.

v0:
```python
import jax
import jax.numpy as jnp
from jax import lax
from jax.sharding import PartitionSpec as P

TOP = 2
CAP = 16


def passed_along(value, axis, by):
    length = lax.axis_size(axis)
    pairs = [(i, i + by) for i in range(length) if 0 <= i + by < length]
    return lax.ppermute(value, axis, pairs)


def build_maps(route_ids, route_gates, experts, rows_all):
    flat_ids = route_ids.reshape(-1)
    onehot = (flat_ids[:, None] == jnp.arange(experts, dtype=jnp.int32)[None, :]).astype(jnp.int32)
    before = jnp.cumsum(onehot, axis=0) - onehot
    placed = flat_ids * CAP + jnp.sum(before * onehot, axis=1)
    matches = jnp.arange(rows_all, dtype=jnp.int32)[:, None] == placed[None, :]
    dispatch_map = jnp.sum(matches.astype(jnp.float32).reshape(rows_all, -1, TOP), axis=2).astype(
        jnp.bfloat16
    )
    combine_map = jnp.sum(
        jnp.where(matches, route_gates.reshape(-1)[None, :], 0.0).reshape(rows_all, -1, TOP), axis=2
    )
    return (dispatch_map, combine_map)


def per_device(tokens, expert_ids, gates, w_gate, w_up, w_down):
    experts = lax.axis_size("expert")
    dp_size = lax.axis_size("dp")
    sections = lax.axis_size("pipe")
    micro_count = tokens.shape[0]
    tok_rows = tokens.shape[1]
    model_width = tokens.shape[2]
    unit_count = w_gate.shape[3]
    columns = model_width // dp_size
    rows_all = experts * CAP
    gate_local = w_gate[0, 0]
    up_local = w_up[0, 0]
    down_local = w_down[0, 0]
    section = lax.axis_index("pipe")
    is_first = section == 0
    column_start = lax.axis_index("dp") * columns
    outputs = jnp.zeros((1, micro_count, tok_rows, columns), jnp.bfloat16)
    carried = jnp.zeros((tok_rows, model_width), jnp.bfloat16)
    turns = micro_count + sections - 1
    for moment in range(turns):
        offset_micro = moment - section
        in_window = (offset_micro >= 0) & (offset_micro < micro_count)
        micro_index = jnp.clip(offset_micro, 0, micro_count - 1)
        own_rows = tokens[min(moment, micro_count - 1)]
        route_ids = lax.dynamic_index_in_dim(expert_ids[0], micro_index, 0, keepdims=False)
        route_gates = lax.dynamic_index_in_dim(gates[0], micro_index, 0, keepdims=False)
        dispatch_map, combine_map = build_maps(route_ids, route_gates, experts, rows_all)
        current = jnp.where(is_first, own_rows, carried)
        current_cols = lax.dynamic_slice_in_dim(current, column_start, columns, 1)
        outgoing = jnp.dot(dispatch_map, current, preferred_element_type=jnp.float32)
        outgoing = outgoing.astype(jnp.bfloat16).reshape(experts, CAP, model_width)
        arrived = lax.all_to_all(outgoing, "expert", split_axis=0, concat_axis=0, tiled=True)
        flat_rows = arrived.reshape(-1, model_width)
        squares = jnp.mean(jnp.square(flat_rows.astype(jnp.float32)), axis=1, keepdims=True)
        inv_rms = lax.rsqrt(squares + 1e-05)
        gate_act = jnp.dot(flat_rows, gate_local, preferred_element_type=jnp.float32) * inv_rms
        up_act = jnp.dot(flat_rows, up_local, preferred_element_type=jnp.float32) * inv_rms
        hidden_rows = (jax.nn.silu(gate_act) * up_act).astype(jnp.bfloat16)
        hidden = hidden_rows.reshape(arrived.shape[0], arrived.shape[1], unit_count)
        hidden = hidden.reshape(rows_all, unit_count)
        summed = lax.psum_scatter(
            lax.dot_general(
                down_local, hidden, (((0,), (1,)), ((), ())), preferred_element_type=jnp.float32
            ),
            "dp",
            scatter_dimension=0,
            tiled=True,
        )
        shares = summed.astype(jnp.bfloat16).reshape(columns, experts, CAP)
        returned = lax.all_to_all(
            shares, "expert", split_axis=1, concat_axis=1, tiled=True
        ).reshape(columns, rows_all)
        mixed = lax.dot_general(
            combine_map,
            returned.astype(jnp.float32),
            (((0,), (1,)), ((), ())),
            precision=lax.Precision.HIGHEST,
            preferred_element_type=jnp.float32,
        )
        new_cols = (current_cols.astype(jnp.float32) + mixed).astype(jnp.bfloat16)
        updated = lax.dynamic_update_slice_in_dim(outputs, new_cols[None, None], micro_index, 1)
        outputs = jnp.where(in_window, updated, outputs)
        if moment + 1 < turns:
            full_rows = lax.all_gather(new_cols, "dp", axis=1, tiled=True)
            carried = passed_along(full_rows, "pipe", 1)
    return outputs


def solution(mesh):
    return jax.shard_map(
        per_device,
        mesh=mesh,
        in_specs=(
            P(None, "expert", None),
            P("pipe", None, "expert", None),
            P("pipe", None, "expert", None),
            P("pipe", "expert", None, "dp"),
            P("pipe", "expert", None, "dp"),
            P("pipe", "expert", "dp", None),
        ),
        out_specs=P("pipe", None, "expert", "dp"),
        check_vma=False,
    )
```

profile of v0, /device:TPU:0, one launch (start us, length us, event | category | flops | bytes accessed | tf_op | source)
XLA Modules:
  0.0 198.9 jit_solution(14078611586446322383)
XLA Ops:
  6.5 0.8 constant_dynamic-slice_fusion
  7.3 0.1 copy.31
  7.4 0.1 eq.95
  7.6 0.1 reduce_window_sum.20
  7.7 0.2 select_reduce_fusion.5
  7.9 0.1 reduce_sum.115
  8.0 0.1 copy.32
  8.1 0.8 fusion.53
  8.8 0.1 convert_reduce_fusion.2
  8.9 0.9 slice_select_fusion
  9.8 0.3 convolution_convert_fusion.2
  10.1 12.1 %all_to_all.30 = bf16[4,16,3072]{2,1,0:T(8,128)(2,1)S(1)} all-to-all(bf16[4,16,3072]{2,1,0:T(8,128)(2,1)S(1)} %bitcast.104), channel_id=1, replica_groups=mesh['dp'=4,'pipe'=2,'expert'=4] {'expert'}, dimensions={0} | all-to-all | bytes 786432 | tf_op jit(solution)/shard_map/all_to_all | solution.py:62
  22.2 0.7 copy-done.3
  23.0 0.1 multiply_reduce_fusion.2
  23.1 0.1 rsqrt.34
  23.2 1.5 convolution_multiply_fusion.5
  24.8 2.8 %convolution_bitcast_fusion.2 = f32[3072,64]{0,1:T(8,128)} fusion(bf16[64,3072]{1,0:T(8,128)(2,1)} %bitcast.99, bf16[1,1,176,3072]{3,2,1,0:T(8,128)(2,1)S(1)} %copy-done, bf16[1,1,3072,176]{2,3,1,0:T(8,128)(2,1)S(1)} %copy-done.2, f32[64,176]{1,0:T(8,128)S(1)} %convolution_multiply_fusion.5, f32[64]{0:T(128)S(1)} %rsqrt.34), kind=kOutput, calls=%fused_computation.2 | convolution fusion | flops 138490880 | bytes 3387648 | tf_op jit(solution)/shard_map/dot_general | solution.py:72
  27.6 0.1 copy.33
  27.7 0.1 eq.102
  28.0 0.2 select_reduce_fusion.3
  28.2 0.1 reduce_sum.120
  28.4 0.1 copy.35
  28.4 0.1 eq.109
  28.7 22.1 %reduce-scatter.4.cloned.1.call-done = f32[768,64]{0,1:T(8,128)} async-done(((f32[3072,64]{0,1:T(8,128)}), f32[768,64]{0,1:T(8,128)}) %reduce-scatter.4.cloned.1.call-update) | async-done | bytes 196624 | tf_op jit(solution)/shard_map/reduce_scatter | solution.py:71
  50.8 1.6 convert_element_type.101
  52.4 3.6 %all-to-all-start.1 = ((bf16[768,4,16]{0,2,1:T(8,128)(2,1)}), bf16[768,4,16]{0,2,1:T(8,128)(2,1)S(1)}, u32[]{:S(2)}, u32[]{:S(2)}) async-start(bf16[768,4,16]{0,2,1:T(8,128)(2,1)} %bitcast.110), calls=%async_computation.2 | async-start | bytes 196608 | tf_op jit(solution)/shard_map/all_to_all | solution.py:80
  56.0 0.2 select_reduce_fusion.1
  56.2 0.1 reduce_sum.125
  56.4 4.6 %all-to-all-done.1 = bf16[768,4,16]{0,2,1:T(8,128)(2,1)S(1)} async-done(((bf16[768,4,16]{0,2,1:T(8,128)(2,1)}), bf16[768,4,16]{0,2,1:T(8,128)(2,1)S(1)}, u32[]{:S(2)}, u32[]{:S(2)}) %all-to-all-start.1) | async-done | bytes 98336 | tf_op jit(solution)/shard_map/all_to_all | solution.py:80
  61.0 0.2 bitcast_dynamic-update-slice_fusion
  61.2 13.5 %all_gather.6 = bf16[24,3072]{1,0:T(8,128)(2,1)S(1)} all-gather(bf16[24,768]{1,0:T(8,128)(2,1)S(1)} %get-tuple-element.20), channel_id=1, replica_groups=mesh['dp'=4,'pipe'=2,'expert'=4] {'dp'}, dimensions={1}, use_global_device_ids=true | all-gather | bytes 184320 | tf_op jit(solution)/shard_map/all_gather | solution.py:94
  74.6 1.3 collective-permute-start
  75.9 0.1 convert_reduce_fusion.1
  76.0 0.9 collective-permute-done
  76.9 0.9 bitcast_select_fusion.1
  77.8 0.3 convolution_convert_fusion.1
  78.1 10.3 %all_to_all.31 = bf16[4,16,3072]{2,1,0:T(8,128)(2,1)S(1)} all-to-all(bf16[4,16,3072]{2,1,0:T(8,128)(2,1)S(1)} %bitcast.105), channel_id=1, replica_groups=mesh['dp'=4,'pipe'=2,'expert'=4] {'expert'}, dimensions={0} | all-to-all | bytes 786432 | tf_op jit(solution)/shard_map/all_to_all | solution.py:62
  88.5 0.7 copy-done.4
  89.2 0.1 multiply_reduce_fusion.1
  89.4 0.1 rsqrt.36
  89.5 1.5 convolution_multiply_fusion.3
  90.9 2.8 %convolution_bitcast_fusion.1 = f32[3072,64]{0,1:T(8,128)} fusion(bf16[64,3072]{1,0:T(8,128)(2,1)} %bitcast.101, bf16[1,1,176,3072]{3,2,1,0:T(8,128)(2,1)S(1)} %copy-done, bf16[1,1,3072,176]{2,3,1,0:T(8,128)(2,1)S(1)} %copy-done.2, f32[64,176]{1,0:T(8,128)S(1)} %convolution_multiply_fusion.3, f32[64]{0:T(128)S(1)} %rsqrt.36), kind=kOutput, calls=%fused_computation.1 | convolution fusion | flops 138490880 | bytes 3387648 | tf_op jit(solution)/shard_map/dot_general | solution.py:72
  93.8 21.2 %reduce-scatter.6.cloned.1.call-done = f32[768,64]{0,1:T(8,128)} async-done(((f32[3072,64]{0,1:T(8,128)}), f32[768,64]{0,1:T(8,128)}) %reduce-scatter.6.cloned.1.call-update) | async-done | bytes 196624 | tf_op jit(solution)/shard_map/reduce_scatter | solution.py:71
  115.1 1.6 convert_element_type.110
  116.6 3.7 %all-to-all-start.3 = ((bf16[768,4,16]{0,2,1:T(8,128)(2,1)}), bf16[768,4,16]{0,2,1:T(8,128)(2,1)S(1)}, u32[]{:S(2)}, u32[]{:S(2)}) async-start(bf16[768,4,16]{0,2,1:T(8,128)(2,1)} %bitcast.111), calls=%async_computation.5 | async-start | bytes 196608 | tf_op jit(solution)/shard_map/all_to_all | solution.py:80
  120.3 4.9 %all-to-all-done.3 = bf16[768,4,16]{0,2,1:T(8,128)(2,1)S(1)} async-done(((bf16[768,4,16]{0,2,1:T(8,128)(2,1)}), bf16[768,4,16]{0,2,1:T(8,128)(2,1)S(1)}, u32[]{:S(2)}, u32[]{:S(2)}) %all-to-all-start.3) | async-done | bytes 98336 | tf_op jit(solution)/shard_map/all_to_all | solution.py:80
  125.2 1.6 fusion.38
  126.8 13.4 %all_gather.7 = bf16[24,3072]{1,0:T(8,128)(2,1)S(1)} all-gather(bf16[24,768]{1,0:T(8,128)(2,1)S(1)} %get-tuple-element.12), channel_id=1, replica_groups=mesh['dp'=4,'pipe'=2,'expert'=4] {'dp'}, dimensions={1}, use_global_device_ids=true | all-gather | bytes 184320 | tf_op jit(solution)/shard_map/all_gather | solution.py:94
  140.2 1.3 collective-permute-start.1
  141.5 0.1 convert_reduce_fusion
  141.5 0.9 collective-permute-done.1
  142.4 0.9 bitcast_select_fusion
  143.4 0.3 convolution_convert_fusion
  143.7 10.3 %all_to_all.32 = bf16[4,16,3072]{2,1,0:T(8,128)(2,1)S(1)} all-to-all(bf16[4,16,3072]{2,1,0:T(8,128)(2,1)S(1)} %bitcast.106), channel_id=1, replica_groups=mesh['dp'=4,'pipe'=2,'expert'=4] {'expert'}, dimensions={0} | all-to-all | bytes 786432 | tf_op jit(solution)/shard_map/all_to_all | solution.py:62
  154.0 0.7 copy-done.5
  154.7 0.1 multiply_reduce_fusion
  154.9 0.1 rsqrt.38
  155.0 1.5 convolution_multiply_fusion.1
  156.5 2.9 %convolution_bitcast_fusion = f32[3072,64]{0,1:T(8,128)} fusion(bf16[64,3072]{1,0:T(8,128)(2,1)} %bitcast.103, bf16[1,1,176,3072]{3,2,1,0:T(8,128)(2,1)S(1)} %copy-done, bf16[1,1,3072,176]{2,3,1,0:T(8,128)(2,1)S(1)} %copy-done.2, f32[64,176]{1,0:T(8,128)S(1)} %convolution_multiply_fusion.1, f32[64]{0:T(128)S(1)} %rsqrt.38), kind=kOutput, calls=%fused_computation | convolution fusion | flops 138490880 | bytes 3387648 | tf_op jit(solution)/shard_map/dot_general | solution.py:72
  159.3 21.3 %reduce-scatter.8.cloned.1.call-done = f32[768,64]{0,1:T(8,128)} async-done(((f32[3072,64]{0,1:T(8,128)}), f32[768,64]{0,1:T(8,128)}) %reduce-scatter.8.cloned.1.call-update) | async-done | bytes 196624 | tf_op jit(solution)/shard_map/reduce_scatter | solution.py:71
  180.7 1.6 convert_element_type.119
  182.2 3.7 %all-to-all-start.5 = ((bf16[768,4,16]{0,2,1:T(8,128)(2,1)}), bf16[768,4,16]{0,2,1:T(8,128)(2,1)S(1)}, u32[]{:S(2)}, u32[]{:S(2)}) async-start(bf16[768,4,16]{0,2,1:T(8,128)(2,1)} %bitcast.27), calls=%async_computation.8 | async-start | bytes 196608 | tf_op jit(solution)/shard_map/all_to_all | solution.py:80
  185.9 4.9 %all-to-all-done.5 = bf16[768,4,16]{0,2,1:T(8,128)(2,1)S(1)} async-done(((bf16[768,4,16]{0,2,1:T(8,128)(2,1)}), bf16[768,4,16]{0,2,1:T(8,128)(2,1)S(1)}, u32[]{:S(2)}, u32[]{:S(2)}) %all-to-all-start.5) | async-done | bytes 98336 | tf_op jit(solution)/shard_map/all_to_all | solution.py:80
  190.8 1.6 fusion.37
  (30 shorter events, 0.7 us)
Async XLA Ops:
  6.5 18.2 %copy-start = (bf16[1,1,176,3072]{3,2,1,0:T(8,128)(2,1)S(1)}, bf16[1,1,176,3072]{3,2,1,0:T(8,128)(2,1)}, u32[]{:S(2)}) copy-start(bf16[1,1,176,3072]{3,2,1,0:T(8,128)(2,1)} %param.11) | copy-start | bytes 3244036
  6.5 44.3 %reduce-scatter.4.cloned.1.call-start = ((), (), s32[]{:S(2)}) async-start(), calls=%async_computation.9 | async-start | bytes 983040 | tf_op jit(solution)/shard_map/reduce_scatter | solution.py:71
  7.6 15.6 %copy-start.1 = (bf16[1,1,3072,176]{2,3,1,0:T(8,128)(2,1)S(1)}, bf16[1,1,3072,176]{2,3,1,0:T(8,128)(2,1)}, u32[]{:S(2)}) copy-start(bf16[1,1,3072,176]{2,3,1,0:T(8,128)(2,1)} %param.9) | copy-start | bytes 3244036
  22.2 0.7 copy-start.3
  23.0 1.8 copy-start.2
  52.4 8.6 %all-to-all-start.1 = ((bf16[768,4,16]{0,2,1:T(8,128)(2,1)}), bf16[768,4,16]{0,2,1:T(8,128)(2,1)S(1)}, u32[]{:S(2)}, u32[]{:S(2)}) async-start(bf16[768,4,16]{0,2,1:T(8,128)(2,1)} %bitcast.110), calls=%async_computation.2 | async-start | bytes 196608 | tf_op jit(solution)/shard_map/all_to_all | solution.py:80
  56.0 59.0 %reduce-scatter.6.cloned.1.call-start = ((), (), s32[]{:S(2)}) async-start(), calls=%async_computation.10 | async-start | bytes 983040 | tf_op jit(solution)/shard_map/reduce_scatter | solution.py:71
  61.2 16.7 %copy-start.6 = (bf16[1,2,24,768]{3,2,1,0:T(8,128)(2,1)}, bf16[1,2,24,768]{3,2,1,0:T(8,128)(2,1)S(1)}, u32[]{:S(2)}) copy-start(bf16[1,2,24,768]{3,2,1,0:T(8,128)(2,1)S(1)} %get-tuple-element.19) | copy-start | bytes 221188
  74.6 2.3 %collective-permute-start = (bf16[24,3072]{1,0:T(8,128)(2,1)S(1)}, bf16[24,3072]{1,0:T(8,128)(2,1)S(1)}, u32[]{:S(2)}, u32[]{:S(2)}) collective-permute-start(bf16[24,3072]{1,0:T(8,128)(2,1)S(1)} %all_gather.6), channel_id=1, source_target_pairs={{0,4},{1,5},{2,6},{3,7},{8,12},{9,13},{10,14},{11,15},{16,20},{17,... | collective-permute-start | bytes 442376 | tf_op jit(solution)/shard_map/ppermute | solution.py:13
  88.5 0.7 copy-start.4
  116.6 8.6 %all-to-all-start.3 = ((bf16[768,4,16]{0,2,1:T(8,128)(2,1)}), bf16[768,4,16]{0,2,1:T(8,128)(2,1)S(1)}, u32[]{:S(2)}, u32[]{:S(2)}) async-start(bf16[768,4,16]{0,2,1:T(8,128)(2,1)} %bitcast.111), calls=%async_computation.5 | async-start | bytes 196608 | tf_op jit(solution)/shard_map/all_to_all | solution.py:80
  120.3 60.4 %reduce-scatter.8.cloned.1.call-start = ((), (), s32[]{:S(2)}) async-start(), calls=%async_computation.11 | async-start | bytes 983040 | tf_op jit(solution)/shard_map/reduce_scatter | solution.py:71
  140.2 2.3 %collective-permute-start.1 = (bf16[24,3072]{1,0:T(8,128)(2,1)S(1)}, bf16[24,3072]{1,0:T(8,128)(2,1)S(1)}, u32[]{:S(2)}, u32[]{:S(2)}) collective-permute-start(bf16[24,3072]{1,0:T(8,128)(2,1)S(1)} %all_gather.7), channel_id=1, source_target_pairs={{0,4},{1,5},{2,6},{3,7},{8,12},{9,13},{10,14},{11,15},{16,20},{17,... | collective-permute-start | bytes 442376 | tf_op jit(solution)/shard_map/ppermute | solution.py:13
  154.0 0.7 copy-start.5
  182.2 8.6 %all-to-all-start.5 = ((bf16[768,4,16]{0,2,1:T(8,128)(2,1)}), bf16[768,4,16]{0,2,1:T(8,128)(2,1)S(1)}, u32[]{:S(2)}, u32[]{:S(2)}) async-start(bf16[768,4,16]{0,2,1:T(8,128)(2,1)} %bitcast.27), calls=%async_computation.8 | async-start | bytes 196608 | tf_op jit(solution)/shard_map/all_to_all | solution.py:80
Sparse Core Ops, SparseCore 0:
  27.8 23.0 reduce-scatter.3
  93.9 21.0 reduce-scatter.5
  159.5 21.1 reduce-scatter.7
where the time goes:
time: 200 us; the launch traced here: 199 us
  waiting for transfers between devices  81 us (40%)
  blocking collectives  59.6 us (30%)
  matrix products  17.2 us (9%)
  starting transfers between devices  13.5 us (7%)
  between operations  13.3 us (7%)
  other arithmetic  9.16 us (5%)
  local copies, waits for them, and re-layouts  5.17 us (3%)
    reduce_scatter x3, waiting for transfers between devices, per_device(): lax.psum_scatter(lax.dot_general(down_local, hidden, (((0,), (1,)), ((),...  64.7 us
    all_to_all x3, blocking collectives, per_device(): lax.all_to_all(outgoing, 'expert', split_axis=0, concat_axis=0, tiled=True)  32.7 us
    all_gather x2, blocking collectives, per_device(): full_rows = lax.all_gather(new_cols, 'dp', axis=1, tiled=True)  26.9 us
    all_to_all x3, waiting for transfers between devices, per_device(): lax.all_to_all(shares, 'expert', split_axis=1, concat_axis=1, tiled=True)  14.4 us
    all_to_all x3, starting transfers between devices, per_device(): lax.all_to_all(shares, 'expert', split_axis=1, concat_axis=1, tiled=True)  11 us
    dot_general x3, matrix products, per_device(): lax.dot_general(down_local, hidden, (((0,), (1,)), ((), ())), preferred_e...  8.54 us
    convert_element_type x3, other arithmetic, per_device(): shares = summed.astype(jnp.bfloat16).reshape(columns, experts, CAP)  4.68 us
    dot_general x3, matrix products, per_device(): jnp.dot(flat_rows, gate_local, preferred_element_type=jnp.float32) * inv_rms  4.54 us
  transfers between devices with their start and end apart: 8, of which 8 were waited for; matrix products, arithmetic and copies ran while one was open for 1% of the time, Pallas kernels for 0%

commit v1 on v0

--- a/solution.py
+++ b/solution.py
@@ -77,8 +77,11 @@
             tiled=True,
         )
         shares = summed.astype(jnp.bfloat16).reshape(columns, experts, CAP)
-        returned = lax.all_to_all(
-            shares, "expert", split_axis=1, concat_axis=1, tiled=True
+        returned = jnp.concatenate(
+            lax.all_to_all(
+                jnp.stack(jnp.split(shares, lax.axis_size("expert"), axis=1)), "expert", 0, 0
+            ),
+            axis=1,
         ).reshape(columns, rows_all)
         mixed = lax.dot_general(
             combine_map,

time: 200 us -> 200 us (level)
  no operation moved by 1% of the time
where the time goes in v1:
time: 200 us; the launch traced here: 199 us
  waiting for transfers between devices  81 us (40%)
  blocking collectives  59.6 us (30%)
  matrix products  17.2 us (9%)
  starting transfers between devices  13.5 us (7%)
  between operations  13.3 us (7%)
  other arithmetic  9.21 us (5%)
  local copies, waits for them, and re-layouts  5.2 us (3%)
    reduce_scatter x3, waiting for transfers between devices, per_device(): lax.psum_scatter(lax.dot_general(down_local, hidden, (((0,), (1,)), ((),...  64.7 us
    all_to_all x3, blocking collectives, per_device(): lax.all_to_all(outgoing, 'expert', split_axis=0, concat_axis=0, tiled=True)  32.7 us
    all_gather x2, blocking collectives, per_device(): full_rows = lax.all_gather(new_cols, 'dp', axis=1, tiled=True)  26.9 us
    all_to_all x3, waiting for transfers between devices, per_device(): lax.all_to_all(jnp.stack(jnp.split(shares, lax.axis_size('expert'), axis=...  14.4 us
    all_to_all x3, starting transfers between devices, per_device(): lax.all_to_all(jnp.stack(jnp.split(shares, lax.axis_size('expert'), axis=...  10.9 us
    dot_general x3, matrix products, per_device(): lax.dot_general(down_local, hidden, (((0,), (1,)), ((), ())), preferred_e...  8.54 us
    dot_general x3, matrix products, per_device(): jnp.dot(flat_rows, gate_local, preferred_element_type=jnp.float32) * inv_rms  4.54 us
  transfers between devices with their start and end apart: 8, of which 8 were waited for; matrix products, arithmetic and copies ran while one was open for 1% of the time, Pallas kernels for 0%

profile of v1, /device:TPU:0, one launch (start us, length us, event | category | flops | bytes accessed | tf_op | source)
XLA Modules:
  0.0 199.0 jit_solution(8946367668423537628)
XLA Ops:
  6.5 0.8 constant_dynamic-slice_fusion
  7.3 0.1 copy.31
  7.4 0.1 eq.95
  7.7 0.2 select_reduce_fusion.5
  7.9 0.1 reduce_sum.115
  8.1 0.8 fusion.53
  8.9 0.9 slice_select_fusion
  9.8 0.3 convolution_convert_fusion.2
  10.1 12.1 %all_to_all.30 = bf16[4,16,3072]{2,1,0:T(8,128)(2,1)S(1)} all-to-all(bf16[4,16,3072]{2,1,0:T(8,128)(2,1)S(1)} %bitcast.134), channel_id=1, replica_groups=mesh['dp'=4,'pipe'=2,'expert'=4] {'expert'}, dimensions={0} | all-to-all | bytes 786432 | tf_op jit(solution)/shard_map/all_to_all | solution.py:62
  22.2 0.7 copy-done.3
  23.0 0.1 multiply_reduce_fusion.2
  23.1 0.1 rsqrt.34
  23.2 1.5 convolution_multiply_fusion.5
  24.8 2.8 %convolution_bitcast_fusion.2 = f32[3072,64]{0,1:T(8,128)} fusion(bf16[64,3072]{1,0:T(8,128)(2,1)} %bitcast.129, bf16[1,1,176,3072]{3,2,1,0:T(8,128)(2,1)S(1)} %copy-done, bf16[1,1,3072,176]{2,3,1,0:T(8,128)(2,1)S(1)} %copy-done.2, f32[64,176]{1,0:T(8,128)S(1)} %convolution_multiply_fusion.5, f32[64]{0:T(128)S(1)} %rsqrt.34), kind=kOutput, calls=%fused_computation.2 | convolution fusion | flops 138490880 | bytes 3387648 | tf_op jit(solution)/shard_map/dot_general | solution.py:72
  27.6 0.1 copy.33
  27.7 0.1 eq.102
  28.0 0.2 select_reduce_fusion.3
  28.2 0.1 reduce_sum.120
  28.4 0.1 copy.35
  28.4 0.1 eq.109
  28.7 22.1 %reduce-scatter.4.cloned.1.call-done = f32[768,64]{0,1:T(8,128)} async-done(((f32[3072,64]{0,1:T(8,128)}), f32[768,64]{0,1:T(8,128)}) %reduce-scatter.4.cloned.1.call-update) | async-done | bytes 196624 | tf_op jit(solution)/shard_map/reduce_scatter | solution.py:71
  50.8 0.9 convert_element_type.101
  51.8 0.6 pad_maximum_fusion
  52.4 3.6 %all-to-all-start.1 = ((bf16[4,768,1,16]{1,3,2,0:T(8,128)(2,1)}), bf16[4,768,1,16]{1,3,2,0:T(8,128)(2,1)S(1)}, u32[]{:S(2)}, u32[]{:S(2)}) async-start(bf16[4,768,1,16]{1,3,2,0:T(8,128)(2,1)} %pad_maximum_fusion), calls=%async_computation.2 | async-start | bytes 196608 | tf_op jit(solution)/shard_map/all_to_all | solution.py:81
  56.1 0.2 select_reduce_fusion.1
  56.2 0.1 reduce_sum.125
  56.4 4.6 %all-to-all-done.1 = bf16[4,768,1,16]{1,3,2,0:T(8,128)(2,1)S(1)} async-done(((bf16[4,768,1,16]{1,3,2,0:T(8,128)(2,1)}), bf16[4,768,1,16]{1,3,2,0:T(8,128)(2,1)S(1)}, u32[]{:S(2)}, u32[]{:S(2)}) %all-to-all-start.1) | async-done | bytes 98336 | tf_op jit(solution)/shard_map/all_to_all | solution.py:81
  61.0 0.2 bitcast_dynamic-update-slice_fusion
  61.2 13.5 %all_gather.6 = bf16[24,3072]{1,0:T(8,128)(2,1)S(1)} all-gather(bf16[24,768]{1,0:T(8,128)(2,1)S(1)} %get-tuple-element.32), channel_id=1, replica_groups=mesh['dp'=4,'pipe'=2,'expert'=4] {'dp'}, dimensions={1}, use_global_device_ids=true | all-gather | bytes 184320 | tf_op jit(solution)/shard_map/all_gather | solution.py:97
  74.7 1.3 collective-permute-start
  76.0 0.1 convert_reduce_fusion.1
  76.1 0.9 collective-permute-done
  76.9 0.9 bitcast_select_fusion.1
  77.9 0.3 convolution_convert_fusion.1
  78.2 10.3 %all_to_all.31 = bf16[4,16,3072]{2,1,0:T(8,128)(2,1)S(1)} all-to-all(bf16[4,16,3072]{2,1,0:T(8,128)(2,1)S(1)} %bitcast.135), channel_id=1, replica_groups=mesh['dp'=4,'pipe'=2,'expert'=4] {'expert'}, dimensions={0} | all-to-all | bytes 786432 | tf_op jit(solution)/shard_map/all_to_all | solution.py:62
  88.5 0.7 copy-done.4
  89.2 0.1 multiply_reduce_fusion.1
  89.4 0.1 rsqrt.36
  89.5 1.5 convolution_multiply_fusion.3
  91.0 2.8 %convolution_bitcast_fusion.1 = f32[3072,64]{0,1:T(8,128)} fusion(bf16[64,3072]{1,0:T(8,128)(2,1)} %bitcast.131, bf16[1,1,176,3072]{3,2,1,0:T(8,128)(2,1)S(1)} %copy-done, bf16[1,1,3072,176]{2,3,1,0:T(8,128)(2,1)S(1)} %copy-done.2, f32[64,176]{1,0:T(8,128)S(1)} %convolution_multiply_fusion.3, f32[64]{0:T(128)S(1)} %rsqrt.36), kind=kOutput, calls=%fused_computation.1 | convolution fusion | flops 138490880 | bytes 3387648 | tf_op jit(solution)/shard_map/dot_general | solution.py:72
  93.9 21.2 %reduce-scatter.6.cloned.1.call-done = f32[768,64]{0,1:T(8,128)} async-done(((f32[3072,64]{0,1:T(8,128)}), f32[768,64]{0,1:T(8,128)}) %reduce-scatter.6.cloned.1.call-update) | async-done | bytes 196624 | tf_op jit(solution)/shard_map/reduce_scatter | solution.py:71
  115.1 0.9 convert_element_type.110
  116.1 0.6 pad_maximum_fusion.1
  116.7 3.7 %all-to-all-start.3 = ((bf16[4,768,1,16]{1,3,2,0:T(8,128)(2,1)}), bf16[4,768,1,16]{1,3,2,0:T(8,128)(2,1)S(1)}, u32[]{:S(2)}, u32[]{:S(2)}) async-start(bf16[4,768,1,16]{1,3,2,0:T(8,128)(2,1)} %pad_maximum_fusion.1), calls=%async_computation.5 | async-start | bytes 196608 | tf_op jit(solution)/shard_map/all_to_all | solution.py:81
  120.4 4.9 %all-to-all-done.3 = bf16[4,768,1,16]{1,3,2,0:T(8,128)(2,1)S(1)} async-done(((bf16[4,768,1,16]{1,3,2,0:T(8,128)(2,1)}), bf16[4,768,1,16]{1,3,2,0:T(8,128)(2,1)S(1)}, u32[]{:S(2)}, u32[]{:S(2)}) %all-to-all-start.3) | async-done | bytes 98336 | tf_op jit(solution)/shard_map/all_to_all | solution.py:81
  125.3 1.6 fusion.38
  126.8 13.4 %all_gather.7 = bf16[24,3072]{1,0:T(8,128)(2,1)S(1)} all-gather(bf16[24,768]{1,0:T(8,128)(2,1)S(1)} %get-tuple-element.12), channel_id=1, replica_groups=mesh['dp'=4,'pipe'=2,'expert'=4] {'dp'}, dimensions={1}, use_global_device_ids=true | all-gather | bytes 184320 | tf_op jit(solution)/shard_map/all_gather | solution.py:97
  140.2 1.3 collective-permute-start.1
  141.5 0.1 convert_reduce_fusion
  141.6 0.9 collective-permute-done.1
  142.5 0.9 bitcast_select_fusion
  143.5 0.3 convolution_convert_fusion
  143.8 10.3 %all_to_all.32 = bf16[4,16,3072]{2,1,0:T(8,128)(2,1)S(1)} all-to-all(bf16[4,16,3072]{2,1,0:T(8,128)(2,1)S(1)} %bitcast.136), channel_id=1, replica_groups=mesh['dp'=4,'pipe'=2,'expert'=4] {'expert'}, dimensions={0} | all-to-all | bytes 786432 | tf_op jit(solution)/shard_map/all_to_all | solution.py:62
  154.1 0.7 copy-done.5
  154.8 0.1 multiply_reduce_fusion
  155.0 0.1 rsqrt.38
  155.1 1.5 convolution_multiply_fusion.1
  156.6 2.8 %convolution_bitcast_fusion = f32[3072,64]{0,1:T(8,128)} fusion(bf16[64,3072]{1,0:T(8,128)(2,1)} %bitcast.133, bf16[1,1,176,3072]{3,2,1,0:T(8,128)(2,1)S(1)} %copy-done, bf16[1,1,3072,176]{2,3,1,0:T(8,128)(2,1)S(1)} %copy-done.2, f32[64,176]{1,0:T(8,128)S(1)} %convolution_multiply_fusion.1, f32[64]{0:T(128)S(1)} %rsqrt.38), kind=kOutput, calls=%fused_computation | convolution fusion | flops 138490880 | bytes 3387648 | tf_op jit(solution)/shard_map/dot_general | solution.py:72
  159.4 21.3 %reduce-scatter.8.cloned.1.call-done = f32[768,64]{0,1:T(8,128)} async-done(((f32[3072,64]{0,1:T(8,128)}), f32[768,64]{0,1:T(8,128)}) %reduce-scatter.8.cloned.1.call-update) | async-done | bytes 196624 | tf_op jit(solution)/shard_map/reduce_scatter | solution.py:71
  180.8 0.9 convert_element_type.119
  181.7 0.6 pad_maximum_fusion.2
  182.4 3.6 %all-to-all-start.5 = ((bf16[4,768,1,16]{1,3,2,0:T(8,128)(2,1)}), bf16[4,768,1,16]{1,3,2,0:T(8,128)(2,1)S(1)}, u32[]{:S(2)}, u32[]{:S(2)}) async-start(bf16[4,768,1,16]{1,3,2,0:T(8,128)(2,1)} %pad_maximum_fusion.2), calls=%async_computation.8 | async-start | bytes 196608 | tf_op jit(solution)/shard_map/all_to_all | solution.py:81
  186.0 4.9 %all-to-all-done.5 = bf16[4,768,1,16]{1,3,2,0:T(8,128)(2,1)S(1)} async-done(((bf16[4,768,1,16]{1,3,2,0:T(8,128)(2,1)}), bf16[4,768,1,16]{1,3,2,0:T(8,128)(2,1)S(1)}, u32[]{:S(2)}, u32[]{:S(2)}) %all-to-all-start.5) | async-done | bytes 98336 | tf_op jit(solution)/shard_map/all_to_all | solution.py:81
  190.9 1.6 fusion.37
  (36 shorter events, 0.9 us)
Async XLA Ops:
  6.5 18.2 %copy-start = (bf16[1,1,176,3072]{3,2,1,0:T(8,128)(2,1)S(1)}, bf16[1,1,176,3072]{3,2,1,0:T(8,128)(2,1)}, u32[]{:S(2)}) copy-start(bf16[1,1,176,3072]{3,2,1,0:T(8,128)(2,1)} %param.11) | copy-start | bytes 3244036
  6.5 44.3 %reduce-scatter.4.cloned.1.call-start = ((), (), s32[]{:S(2)}) async-start(), calls=%async_computation.9 | async-start | bytes 983040 | tf_op jit(solution)/shard_map/reduce_scatter | solution.py:71
  7.6 15.6 %copy-start.1 = (bf16[1,1,3072,176]{2,3,1,0:T(8,128)(2,1)S(1)}, bf16[1,1,3072,176]{2,3,1,0:T(8,128)(2,1)}, u32[]{:S(2)}) copy-start(bf16[1,1,3072,176]{2,3,1,0:T(8,128)(2,1)} %param.9) | copy-start | bytes 3244036
  22.2 0.7 copy-start.3
  23.0 1.8 copy-start.2
  52.4 8.6 %all-to-all-start.1 = ((bf16[4,768,1,16]{1,3,2,0:T(8,128)(2,1)}), bf16[4,768,1,16]{1,3,2,0:T(8,128)(2,1)S(1)}, u32[]{:S(2)}, u32[]{:S(2)}) async-start(bf16[4,768,1,16]{1,3,2,0:T(8,128)(2,1)} %pad_maximum_fusion), calls=%async_computation.2 | async-start | bytes 196608 | tf_op jit(solution)/shard_map/all_to_all | solution.py:81
  56.1 59.0 %reduce-scatter.6.cloned.1.call-start = ((), (), s32[]{:S(2)}) async-start(), calls=%async_computation.10 | async-start | bytes 983040 | tf_op jit(solution)/shard_map/reduce_scatter | solution.py:71
  61.2 16.7 %copy-start.6 = (bf16[1,2,24,768]{3,2,1,0:T(8,128)(2,1)}, bf16[1,2,24,768]{3,2,1,0:T(8,128)(2,1)S(1)}, u32[]{:S(2)}) copy-start(bf16[1,2,24,768]{3,2,1,0:T(8,128)(2,1)S(1)} %get-tuple-element.31) | copy-start | bytes 221188
  74.7 2.3 %collective-permute-start = (bf16[24,3072]{1,0:T(8,128)(2,1)S(1)}, bf16[24,3072]{1,0:T(8,128)(2,1)S(1)}, u32[]{:S(2)}, u32[]{:S(2)}) collective-permute-start(bf16[24,3072]{1,0:T(8,128)(2,1)S(1)} %all_gather.6), channel_id=1, source_target_pairs={{0,4},{1,5},{2,6},{3,7},{8,12},{9,13},{10,14},{11,15},{16,20},{17,... | collective-permute-start | bytes 442376 | tf_op jit(solution)/shard_map/ppermute | solution.py:13
  88.5 0.7 copy-start.4
  116.7 8.6 %all-to-all-start.3 = ((bf16[4,768,1,16]{1,3,2,0:T(8,128)(2,1)}), bf16[4,768,1,16]{1,3,2,0:T(8,128)(2,1)S(1)}, u32[]{:S(2)}, u32[]{:S(2)}) async-start(bf16[4,768,1,16]{1,3,2,0:T(8,128)(2,1)} %pad_maximum_fusion.1), calls=%async_computation.5 | async-start | bytes 196608 | tf_op jit(solution)/shard_map/all_to_all | solution.py:81
  120.4 60.4 %reduce-scatter.8.cloned.1.call-start = ((), (), s32[]{:S(2)}) async-start(), calls=%async_computation.11 | async-start | bytes 983040 | tf_op jit(solution)/shard_map/reduce_scatter | solution.py:71
  140.2 2.3 %collective-permute-start.1 = (bf16[24,3072]{1,0:T(8,128)(2,1)S(1)}, bf16[24,3072]{1,0:T(8,128)(2,1)S(1)}, u32[]{:S(2)}, u32[]{:S(2)}) collective-permute-start(bf16[24,3072]{1,0:T(8,128)(2,1)S(1)} %all_gather.7), channel_id=1, source_target_pairs={{0,4},{1,5},{2,6},{3,7},{8,12},{9,13},{10,14},{11,15},{16,20},{17,... | collective-permute-start | bytes 442376 | tf_op jit(solution)/shard_map/ppermute | solution.py:13
  154.1 0.7 copy-start.5
  182.4 8.5 %all-to-all-start.5 = ((bf16[4,768,1,16]{1,3,2,0:T(8,128)(2,1)}), bf16[4,768,1,16]{1,3,2,0:T(8,128)(2,1)S(1)}, u32[]{:S(2)}, u32[]{:S(2)}) async-start(bf16[4,768,1,16]{1,3,2,0:T(8,128)(2,1)} %pad_maximum_fusion.2), calls=%async_computation.8 | async-start | bytes 196608 | tf_op jit(solution)/shard_map/all_to_all | solution.py:81
Sparse Core Ops, SparseCore 0:
  27.8 23.0 reduce-scatter.3
  94.0 21.0 reduce-scatter.5
  159.6 21.1 reduce-scatter.7
